TPU v7x, 512 devices: a whole 4x4x16 slice. The times are simulated.
512 devices in a mesh: seq: 64 (over z, y), tensor: 8 (over x, core).
Axes of the slice: x: 4, y: 4, z: 16, core: 2. Of those that a mesh axis runs over, the one named last changes fastest.
Arguments:
- hidden: bfloat16 [8192, 4096], P('seq', 'tensor')
- norm_gain: bfloat16 [4096], replicated, may hold values from 0.5 to 1.5
- w_query: bfloat16 [4096, 4096], P('seq', 'tensor')
- key_value_weight: bfloat16 [4096, 1024], P('seq')
- w_out: bfloat16 [4096, 4096], P('tensor', 'seq'), may hold values from -0.09375 to 0.09375
- prefix_key_cache: bfloat16 [64, 1024, 1024], P('seq')
- prefix_owner: int32 [64], replicated, may hold values from 0 to 63, each once
- token_counts: int32 [64, 64], P('seq'), may hold values from 0 to 4, as said below
Outputs:
- attn_out: bfloat16 [8192, 4096], P('seq', 'tensor')
- suffix_key_cache: bfloat16 [8192, 1024], P('seq', 'tensor')
Inputs may be any that keep to these rules, and one draw needn't show every extreme that they name: `token_counts`: each row sums to 128; one prefix receives exactly 4 tokens from every sequence index.
All inputs are finite; a program needn't handle non-finite values.
Results may differ from a plain program's by a relative error of at most 0.035.
Values may be sent and summed in bfloat16 or wider, within the bound.
No kernel may reach another device: no remote copies, remote signals or barrier semaphores. Data moves between devices by JAX's collectives and lax.ppermute only.
A program may use at most 64 MiB of HBM per device.

v0:
```python
import jax
import jax.numpy as jnp
from jax import lax
from jax.sharding import PartitionSpec as P

HEAD_DIM = 128
PREFIX_LENGTH = 1024
eps = 1e-06
theta = 5000000.0


def rotate(values, positions):
    half = values.shape[-1] // 2
    frequency = theta ** (-jnp.arange(half, dtype=jnp.float32) * 2.0 / values.shape[-1])
    angle = positions.astype(jnp.float32)[:, None] * frequency[None, :]
    cosine = jnp.cos(angle)[:, None, :]
    sine = jnp.sin(angle)[:, None, :]
    first = values[..., :half]
    second = values[..., half:]
    return jnp.concatenate(
        [first * cosine - second * sine, second * cosine + first * sine], axis=-1
    )


def layout(counts_row, length):
    ends = jnp.cumsum(counts_row)
    starts = ends - counts_row
    places = jnp.arange(length, dtype=jnp.int32)
    member = (places[:, None] >= starts[None, :]) & (places[:, None] < ends[None, :])
    labels = jnp.arange(counts_row.shape[0], dtype=jnp.int32)
    prefix_group = jnp.sum(jnp.where(member, labels[None, :], 0), axis=1)
    offset = places - jnp.sum(jnp.where(member, starts[None, :], 0), axis=1)
    return (starts, prefix_group, offset)


def attend(query_vectors, keys, values, allowed):
    scores = lax.dot_general(
        query_vectors, keys, (((1,), (1,)), ((), ())), preferred_element_type=jnp.float32
    )
    scores = scores * (1.0 / query_vectors.shape[-1] ** 0.5)
    if allowed is not None:
        scores = jnp.where(allowed, scores, -1e30)
    top = jnp.max(scores, axis=1, keepdims=True)
    expo = jnp.exp(scores - top)
    total = jnp.sum(expo, axis=1, keepdims=True)
    weights = (expo / total).astype(jnp.bfloat16)
    result = jnp.dot(weights, values, preferred_element_type=jnp.float32)
    return (result, top[:, 0] + jnp.log(total[:, 0]))


def shards(
    hidden,
    norm_gain,
    w_query,
    key_value_weight,
    w_out,
    prefix_key_cache,
    prefix_owner,
    token_counts,
):
    tensor_index = lax.axis_index("tensor")
    tensor_count = lax.axis_size("tensor")
    seq_count = lax.axis_size("seq")
    length = hidden.shape[0]
    head_size = HEAD_DIM
    whole = lax.all_gather(hidden, "tensor", axis=1, tiled=True)
    wide = whole.astype(jnp.float32)
    normalized_input = (
        wide
        * lax.rsqrt(jnp.mean(wide * wide, axis=1, keepdims=True) + eps)
        * norm_gain.astype(jnp.float32)
    ).astype(jnp.bfloat16)
    width_query = w_query.shape[1]
    full_width = key_value_weight.shape[1]
    heads_dev = width_query // head_size
    kv_heads = full_width // (2 * head_size)

    def contract(piece):
        return jnp.dot(normalized_input, piece, preferred_element_type=jnp.float32)

    query_vectors = contract(lax.all_gather(w_query, "seq", axis=0, tiled=True))
    key_value_pair = contract(lax.all_gather(key_value_weight, "seq", axis=0, tiled=True))
    counts = token_counts[0]
    num_groups = counts.shape[0]
    starts, prefix_group, offset = layout(counts, length)
    positions = PREFIX_LENGTH + offset
    query_vectors = rotate(query_vectors.reshape(length, heads_dev, head_size), positions).astype(
        jnp.bfloat16
    )
    pair_blocks = key_value_pair.reshape(length, kv_heads, 2, head_size)
    rotated_keys = rotate(pair_blocks[:, :, 0], positions)
    pair_all = jnp.stack([rotated_keys, pair_blocks[:, :, 1]], axis=2).astype(jnp.bfloat16)
    suffix_full = pair_all.reshape(length, full_width)
    share = full_width // tensor_count
    suffix_part = lax.dynamic_slice_in_dim(suffix_full, tensor_index * share, share, 1)
    group_full = heads_dev * tensor_count // kv_heads
    kv_local = max(1, heads_dev // group_full)
    kv_start = tensor_index * heads_dev // group_full
    suffix_mine = lax.dynamic_slice_in_dim(pair_all, kv_start, kv_local, 1)
    suffix_keys = suffix_mine[:, :, 0]
    suffix_values = suffix_mine[:, :, 1]
    cache_all = prefix_key_cache[0].reshape(-1, kv_heads, 2, head_size)
    cache_mine = lax.dynamic_slice_in_dim(cache_all, kv_start, kv_local, 1)
    cache_keys = cache_mine[:, :, 0]
    cache_values = cache_mine[:, :, 1]
    group_width = heads_dev // kv_local
    capacity = 2 * length // seq_count
    labels = jnp.arange(num_groups, dtype=jnp.int32)
    owner_match = prefix_owner[None, :] == jnp.arange(seq_count, dtype=jnp.int32)[:, None]
    owner_start = jnp.sum(jnp.where(owner_match, starts[None, :], 0), axis=1)
    owner_count = jnp.sum(jnp.where(owner_match, counts[None, :], 0), axis=1)
    slots = jnp.arange(capacity, dtype=jnp.int32)
    valid = slots[None, :] < owner_count[:, None]
    source_rows = jnp.where(valid, owner_start[:, None] + slots[None, :], 0)
    flat_query = query_vectors.reshape(length, width_query)
    outgoing = jnp.where(valid[:, :, None], flat_query[source_rows], jnp.zeros((), jnp.bfloat16))
    arrived = lax.all_to_all(outgoing, "seq", split_axis=0, concat_axis=0, tiled=True)
    items = arrived.shape[1]
    rows_in = arrived.reshape(seq_count * items, heads_dev, head_size)
    outs = []
    logs = []
    for serve_head in range(heads_dev):
        serve_result, serve_logsum = attend(
            rows_in[:, serve_head],
            cache_keys[:, serve_head // group_width],
            cache_values[:, serve_head // group_width],
            None,
        )
        outs.append(serve_result)
        logs.append(serve_logsum)
    out_block = jnp.stack(outs, axis=1).astype(jnp.bfloat16).reshape(seq_count, items, width_query)
    log_block = jnp.stack(logs, axis=1).reshape(seq_count, items, heads_dev)
    prefix_out = lax.all_to_all(out_block, "seq", split_axis=0, concat_axis=0, tiled=True)
    prefix_log = lax.all_to_all(
        log_block.astype(jnp.bfloat16), "seq", split_axis=0, concat_axis=0, tiled=True
    ).astype(log_block.dtype)
    owner_of_token = jnp.sum(
        jnp.where(prefix_group[:, None] == labels[None, :], prefix_owner[None, :], 0), axis=1
    )
    back_rows = owner_of_token * capacity + offset
    prefix_rows = prefix_out.reshape(seq_count * capacity, heads_dev, head_size)[back_rows]
    prefix_logsum = prefix_log.reshape(seq_count * capacity, heads_dev)[back_rows]
    places = jnp.arange(length, dtype=jnp.int32)
    allowed = (prefix_group[:, None] == prefix_group[None, :]) & (
        places[None, :] <= places[:, None]
    )
    outs = []
    logs = []
    for head in range(heads_dev):
        result, logsum = attend(
            query_vectors[:, head],
            suffix_keys[:, head // group_width],
            suffix_values[:, head // group_width],
            allowed,
        )
        outs.append(result)
        logs.append(logsum)
    suffix_attn = jnp.stack(outs, axis=1)
    suffix_logsum = jnp.stack(logs, axis=1)
    upper = jnp.maximum(prefix_logsum, suffix_logsum)
    left = jnp.exp(prefix_logsum - upper)[..., None]
    right = jnp.exp(suffix_logsum - upper)[..., None]
    context = (
        (left * prefix_rows.astype(jnp.float32) + right * suffix_attn) / (left + right)
    ).astype(jnp.bfloat16)
    context = context.reshape(length, width_query)
    partial_out = jnp.dot(
        context,
        lax.all_gather(w_out, "seq", axis=1, tiled=True),
        preferred_element_type=jnp.float32,
    )
    attn_out = lax.psum_scatter(
        partial_out.astype(jnp.bfloat16), "tensor", scatter_dimension=1, tiled=True
    )
    return (attn_out, suffix_part)


def solution(mesh):
    in_specs = (
        P("seq", "tensor"),
        P(),
        P("seq", "tensor"),
        P("seq", None),
        P("tensor", "seq"),
        P("seq", None, None),
        P(),
        P("seq", None),
    )
    out_specs = (P("seq", "tensor"), P("seq", "tensor"))
    return jax.shard_map(shards, mesh=mesh, in_specs=in_specs, out_specs=out_specs, check_vma=False)
```

profile of v0, /device:TPU:8, one launch (start us, length us, event | category | flops | bytes accessed | tf_op | source)
XLA Modules:
  0.0 541.2 jit_solution(3711993992200430537)
XLA Ops:
  7.2 0.7 all-gather.5.cloned.1.call-update
  7.9 0.7 all-gather.7.cloned.1.call-update
  8.7 0.7 all-gather.9.cloned.1.call-update
  10.0 0.7 convert_element_type.73
  10.7 0.7 copy.120
  11.6 0.7 fusion.63
  12.4 2.9 copy.123
  16.5 1.0 multiply_cosine_fusion
  17.4 28.1 %all-gather.5.cloned.1.call-done = bf16[128,4096]{1,0:T(8,128)(2,1)} async-done(((bf16[128,512]{1,0:T(8,128)(2,1)}), bf16[128,4096]{1,0:T(8,128)(2,1)}) %all-gather.5.cloned.1.call-update) | async-done | bytes 1048592 | tf_op jit(solution)/shard_map/all_gather | solution.py:66
  45.6 1.5 fusion
  47.1 146.7 %all-gather.7.cloned.1.call-done = bf16[4096,512]{1,0:T(8,128)(2,1)} async-done(((bf16[64,512]{1,0:T(8,128)(2,1)}), bf16[4096,512]{1,0:T(8,128)(2,1)}) %all-gather.7.cloned.1.call-update) | async-done | bytes 4194320 | tf_op jit(solution)/shard_map/all_gather | solution.py:81
  193.8 4.0 fusion.17
  197.8 1.0 reshape.549
  198.8 0.9 fusion.69
  199.7 148.7 %all-gather.9.cloned.1.call-done = bf16[4096,1024]{1,0:T(8,128)(2,1)} async-done(((bf16[64,1024]{1,0:T(8,128)(2,1)}), bf16[4096,1024]{1,0:T(8,128)(2,1)}) %all-gather.9.cloned.1.call-update) | async-done | bytes 8388624 | tf_op jit(solution)/shard_map/all_gather | solution.py:82
  348.5 5.5 %fusion.15 = f32[128,1024]{1,0:T(8,128)} fusion(bf16[4096,1024]{1,0:T(8,128)(2,1)} %all-gather.9.cloned.1.call-done, bf16[128,4096]{1,0:T(8,128)(2,1)S(1)} %copy-done, f32[4096]{0:T(1024)S(1)} %convert_element_type.73, f32[128]{0:T(128)S(1)} %add_rsqrt_fusion), kind=kOutput, calls=%fused_computation.46 | convolution fusion | flops 1075838976 | bytes 9978368 | tf_op jit(solution)/shard_map/dot_general | solution.py:79
  354.0 1.5 reshape.555
  356.1 1.1 multiply_subtract_fusion
  357.3 1.2 gather_fusion
  358.5 0.9 broadcast_select_fusion
  359.4 10.4 %all-to-all-start = ((bf16[64,4,512]{2,1,0:T(4,128)(2,1)}), bf16[64,4,512]{2,1,0:T(4,128)(2,1)S(1)}, u32[]{:S(2)}, u32[]{:S(2)}) async-start(bf16[64,4,512]{2,1,0:T(4,128)(2,1)} %broadcast_select_fusion), calls=%async_computation | async-start | bytes 524288 | tf_op jit(solution)/shard_map/all_to_all | solution.py:117
  373.2 0.8 convolution_bitcast_fusion
  374.0 14.2 %all-to-all-done = bf16[64,4,512]{2,1,0:T(4,128)(2,1)S(1)} async-done(((bf16[64,4,512]{2,1,0:T(4,128)(2,1)}), bf16[64,4,512]{2,1,0:T(4,128)(2,1)S(1)}, u32[]{:S(2)}, u32[]{:S(2)}) %all-to-all-start) | async-done | bytes 262176 | tf_op jit(solution)/shard_map/all_to_all | solution.py:117
  388.3 1.1 fusion.68
  391.3 0.8 add.239
  392.1 1.3 fusion.75
  393.4 1.0 copy-done.1
  395.7 1.4 add.237
  397.1 1.3 fusion.76
  398.4 1.0 copy-done.3
  400.9 1.4 add.235
  402.6 1.0 copy-done.5
  404.1 0.8 pad_maximum_fusion.1
  404.8 0.7 copy.125
  405.5 5.5 %all-to-all-start.1 = ((bf16[64,4,4]{1,2,0:T(4,128)(2,1)}), bf16[64,4,4]{1,2,0:T(4,128)(2,1)S(1)}, u32[]{:S(2)}, u32[]{:S(2)}) async-start(bf16[64,4,4]{1,2,0:T(4,128)(2,1)} %copy.125), calls=%async_computation.1 | async-start | bytes 131072 | tf_op jit(solution)/shard_map/all_to_all | solution.py:134
  411.1 1.1 fusion.6
  412.7 0.8 copy-done.4
  413.9 0.8 copy-done.6
  415.5 0.8 convert_element_type.83
  416.3 9.3 %all-to-all-done.1 = bf16[64,4,4]{1,2,0:T(4,128)(2,1)S(1)} async-done(((bf16[64,4,4]{1,2,0:T(4,128)(2,1)}), bf16[64,4,4]{1,2,0:T(4,128)(2,1)S(1)}, u32[]{:S(2)}, u32[]{:S(2)}) %all-to-all-start.1) | async-done | bytes 2080 | tf_op jit(solution)/shard_map/all_to_all | solution.py:134
  425.6 5.9 %all-to-all-start.2 = ((bf16[64,4,512]{2,1,0:T(4,128)(2,1)}), bf16[64,4,512]{2,1,0:T(4,128)(2,1)S(1)}, u32[]{:S(2)}, u32[]{:S(2)}) async-start(bf16[64,4,512]{2,1,0:T(4,128)(2,1)} %convert_element_type.83), calls=%async_computation.2 | async-start | bytes 524288 | tf_op jit(solution)/shard_map/all_to_all | solution.py:133
  432.6 0.8 gather_fusion.1
  433.5 16.1 %all-to-all-done.2 = bf16[64,4,512]{2,1,0:T(4,128)(2,1)S(1)} async-done(((bf16[64,4,512]{2,1,0:T(4,128)(2,1)}), bf16[64,4,512]{2,1,0:T(4,128)(2,1)S(1)}, u32[]{:S(2)}, u32[]{:S(2)}) %all-to-all-start.2) | async-done | bytes 262176 | tf_op jit(solution)/shard_map/all_to_all | solution.py:133
  449.7 0.9 gather_fusion.2
  450.8 44.6 %all-gather.11.cloned.1.call-done = bf16[512,4096]{0,1:T(8,128)(2,1)} async-done(((bf16[512,64]{0,1:T(8,128)(2,1)}), bf16[512,4096]{0,1:T(8,128)(2,1)}) %all-gather.11.cloned.1.call-update) | async-done | bytes 4194320 | tf_op jit(solution)/shard_map/all_gather | solution.py:169
  495.3 4.7 convolution_convert_fusion
  500.2 0.7 copy.137
  500.9 33.8 %reduce-scatter.2.cloned.1.call-done = bf16[128,512]{1,0:T(8,128)(2,1)} async-done(((bf16[128,4096]{1,0:T(8,128)(2,1)}), bf16[128,512]{1,0:T(8,128)(2,1)}) %reduce-scatter.2.cloned.1.call-update) | async-done | bytes 131088 | tf_op jit(solution)/shard_map/reduce_scatter | solution.py:172
  (150 shorter events, 14.9 us)
Async XLA Ops:
  7.2 38.4 %all-gather.5.cloned.1.call-start = ((), (), s32[]{:S(2)}) async-start(), calls=%async_computation.4 | async-start | bytes 1179648 | tf_op jit(solution)/shard_map/all_gather | solution.py:66
  7.9 185.9 %all-gather.7.cloned.1.call-start = ((), (), s32[]{:S(2)}) async-start(), calls=%async_computation.5 | async-start | bytes 4259840 | tf_op jit(solution)/shard_map/all_gather | solution.py:81
  8.6 339.8 %all-gather.9.cloned.1.call-start = ((), (), s32[]{:S(2)}) async-start(), calls=%async_computation.6 | async-start | bytes 8519680 | tf_op jit(solution)/shard_map/all_gather | solution.py:82
  9.4 486.0 %all-gather.11.cloned.1.call-start = ((), (), s32[]{:S(2)}) async-start(), calls=%async_computation.7 | async-start | bytes 4259840 | tf_op jit(solution)/shard_map/all_gather | solution.py:169
  12.4 2.9 copy-start.28
  12.4 2.9 copy-start.42
  47.1 301.4 %copy-start = (bf16[128,4096]{1,0:T(8,128)(2,1)S(1)}, bf16[128,4096]{1,0:T(8,128)(2,1)}, u32[]{:S(2)}) copy-start(bf16[128,4096]{1,0:T(8,128)(2,1)} %all-gather.5.cloned.1.call-done) | copy-start | bytes 3145732
  354.0 2.1 copy-start.7
  354.0 2.1 copy-start.8
  359.4 28.7 %all-to-all-start = ((bf16[64,4,512]{2,1,0:T(4,128)(2,1)}), bf16[64,4,512]{2,1,0:T(4,128)(2,1)S(1)}, u32[]{:S(2)}, u32[]{:S(2)}) async-start(bf16[64,4,512]{2,1,0:T(4,128)(2,1)} %broadcast_select_fusion), calls=%async_computation | async-start | bytes 524288 | tf_op jit(solution)/shard_map/all_to_all | solution.py:117
  370.1 3.9 copy-start.29
  370.3 0.9 copy-start.31
  370.3 19.0 %copy-start.9 = (f32[128,128]{0,1:T(8,128)}, f32[128,128]{0,1:T(8,128)S(1)}, u32[]{:S(2)}) copy-start(f32[128,128]{0,1:T(8,128)S(1)} %get-tuple-element.36) | copy-start | bytes 196612
  370.4 3.6 copy-start.33
  371.2 0.6 copy-start.35
  371.2 18.2 %copy-start.11 = (f32[128,128]{0,1:T(8,128)}, f32[128,128]{0,1:T(8,128)S(1)}, u32[]{:S(2)}) copy-start(f32[128,128]{0,1:T(8,128)S(1)} %get-tuple-element.38) | copy-start | bytes 196612
  372.5 1.5 copy-start.13
  372.5 1.5 copy-start.39
  393.4 1.0 copy-start.1
  393.4 1.3 copy-start.17
  398.3 1.0 copy-start.3
  398.3 1.3 copy-start.19
  399.7 0.6 copy-start.26
  402.6 1.0 copy-start.5
  402.6 1.3 copy-start.21
  405.5 20.1 %all-to-all-start.1 = ((bf16[64,4,4]{1,2,0:T(4,128)(2,1)}), bf16[64,4,4]{1,2,0:T(4,128)(2,1)S(1)}, u32[]{:S(2)}, u32[]{:S(2)}) async-start(bf16[64,4,4]{1,2,0:T(4,128)(2,1)} %copy.125), calls=%async_computation.1 | async-start | bytes 131072 | tf_op jit(solution)/shard_map/all_to_all | solution.py:134
  411.1 1.2 copy-start.2
  411.1 1.2 copy-start.18
  411.1 1.2 copy-start.25
  412.3 1.2 copy-start.4
  412.3 1.2 copy-start.20
  412.3 1.2 copy-start.27
  413.5 1.2 copy-start.6
  413.5 1.2 copy-start.22
  415.1 16.4 %copy-start.10 = (f32[128,128]{0,1:T(8,128)S(1)}, f32[128,128]{0,1:T(8,128)}, u32[]{:S(2)}) copy-start(f32[128,128]{0,1:T(8,128)} %copy-done.9) | copy-start | bytes 196612
  415.2 16.4 %copy-start.32 = (f32[128]{0:T(128)S(1)}, f32[128]{0:T(128)}, u32[]{:S(2)}) copy-start(f32[128]{0:T(128)} %copy-done.31) | copy-start | bytes 1540
  415.2 16.4 %copy-start.37 = (f32[128]{0:T(128)S(1)}, f32[128]{0:T(128)}, u32[]{:S(2)}) copy-start(f32[128]{0:T(128)} %fusion.33) | copy-start | bytes 1540
  415.2 16.6 %copy-start.12 = (f32[128,128]{0,1:T(8,128)S(1)}, f32[128,128]{0,1:T(8,128)}, u32[]{:S(2)}) copy-start(f32[128,128]{0,1:T(8,128)} %copy-done.11) | copy-start | bytes 196612
  415.2 16.6 %copy-start.36 = (f32[128]{0:T(128)S(1)}, f32[128]{0:T(128)}, u32[]{:S(2)}) copy-start(f32[128]{0:T(128)} %copy-done.35) | copy-start | bytes 1540
  415.2 16.6 %copy-start.38 = (f32[128]{0:T(128)S(1)}, f32[128]{0:T(128)}, u32[]{:S(2)}) copy-start(f32[128]{0:T(128)} %fusion.32) | copy-start | bytes 1540
  415.2 16.8 %copy-start.14 = (f32[128,128]{0,1:T(8,128)S(1)}, f32[128,128]{0,1:T(8,128)}, u32[]{:S(2)}) copy-start(f32[128,128]{0,1:T(8,128)} %copy-done.13) | copy-start | bytes 196612
  415.2 16.8 %copy-start.40 = (f32[128]{0:T(128)S(1)}, f32[128]{0:T(128)}, u32[]{:S(2)}) copy-start(f32[128]{0:T(128)} %copy-done.39) | copy-start | bytes 1540
  415.2 16.8 %copy-start.41 = (f32[128]{0:T(128)S(1)}, f32[128]{0:T(128)}, u32[]{:S(2)}) copy-start(f32[128]{0:T(128)} %fusion.31) | copy-start | bytes 1540
  415.2 17.1 %copy-start.30 = (f32[128]{0:T(128)S(1)}, f32[128]{0:T(128)}, u32[]{:S(2)}) copy-start(f32[128]{0:T(128)} %copy-done.29) | copy-start | bytes 1540
  415.2 17.1 %copy-start.34 = (f32[128]{0:T(128)S(1)}, f32[128]{0:T(128)}, u32[]{:S(2)}) copy-start(f32[128]{0:T(128)} %copy-done.33) | copy-start | bytes 1540
  415.3 35.4 %copy-start.15 = (f32[128,1,128]{0,2,1:T(8,128)S(1)}, f32[128,1,128]{0,2,1:T(8,128)}, u32[]{:S(2)}) copy-start(f32[128,1,128]{0,2,1:T(8,128)} %convolution_bitcast_fusion) | copy-start | bytes 196612
  425.6 24.0 %all-to-all-start.2 = ((bf16[64,4,512]{2,1,0:T(4,128)(2,1)}), bf16[64,4,512]{2,1,0:T(4,128)(2,1)S(1)}, u32[]{:S(2)}, u32[]{:S(2)}) async-start(bf16[64,4,512]{2,1,0:T(4,128)(2,1)} %convert_element_type.83), calls=%async_computation.2 | async-start | bytes 524288 | tf_op jit(solution)/shard_map/all_to_all | solution.py:133
  431.5 103.2 %reduce-scatter.2.cloned.1.call-start = ((), (), s32[]{:S(2)}) async-start(), calls=%async_computation.8 | async-start | bytes 1179648 | tf_op jit(solution)/shard_map/reduce_scatter | solution.py:172
  (3 other events, 1.6 us)
Sparse Core Ops, SparseCore 0:
  10.1 35.3 all-gather.4
  48.5 145.2 all-gather.6
  196.7 151.7 all-gather.8
  351.3 144.0 all-gather.10
  500.1 34.5 reduce-scatter.1
where the time goes:
time: 542 us; the launch traced here: 541 us
  waiting for transfers between devices  444 us (82%)
  local copies, waits for them, and re-layouts  25.9 us (5%)
  starting transfers between devices  22 us (4%)
  matrix products  21.8 us (4%)
  between operations  14.5 us (3%)
  other arithmetic  13 us (2%)
    all_gather x1, waiting for transfers between devices, shards(): lax.all_gather(key_value_weight, 'seq', axis=0, tiled=True)  149 us
    all_gather x1, waiting for transfers between devices, shards(): query_vectors = contract(lax.all_gather(w_query, 'seq', axis=0, tiled=True))  147 us
    all_gather x1, waiting for transfers between devices, shards(): lax.all_gather(w_out, 'seq', axis=1, tiled=True)  44.6 us
    reduce_scatter x1, waiting for transfers between devices, shards(): lax.psum_scatter(partial_out.astype(jnp.bfloat16), 'tensor', scatter_dime...  33.8 us
    all_gather x1, waiting for transfers between devices, shards(): whole = lax.all_gather(hidden, 'tensor', axis=1, tiled=True)  28.1 us
    all_to_all x1, waiting for transfers between devices, shards(): lax.all_to_all(out_block, 'seq', split_axis=0, concat_axis=0, tiled=True)  16.1 us
    all_to_all x1, waiting for transfers between devices, shards(): lax.all_to_all(outgoing, 'seq', split_axis=0, concat_axis=0, tiled=True)  14.2 us
    unnamed x90, local copies, waits for them, and re-layouts  10.9 us
  transfers between devices with their start and end apart: 8, of which 8 were waited for; matrix products, arithmetic and copies ran while one was open for 9% of the time, Pallas kernels for 0%

commit v1 on v0

--- a/solution.py
+++ b/solution.py
@@ -79,7 +79,12 @@
         return jnp.dot(normalized_input, piece, preferred_element_type=jnp.float32)
 
     query_vectors = contract(lax.all_gather(w_query, "seq", axis=0, tiled=True))
-    key_value_pair = contract(lax.all_gather(key_value_weight, "seq", axis=0, tiled=True))
+    key_value_pair = contract(
+        jnp.concatenate(
+            lax.all_to_all(jnp.stack([key_value_weight] * lax.axis_size("seq")), "seq", 0, 0),
+            axis=0,
+        )
+    )
     counts = token_counts[0]
     num_groups = counts.shape[0]
     starts, prefix_group, offset = layout(counts, length)

time: 542 us -> 591 us (1.090)
  waiting for transfers between devices: 444 us -> 469 us
  starting transfers between devices: 22 us -> 36.9 us
  local copies, waits for them, and re-layouts: 25.9 us -> 37.9 us
    all_gather x1 -> x0, waiting for transfers between devices: 149 us -> none  [shards(): lax.all_gather(key_value_weight, 'seq', axis=0, tiled=True)]
    all_to_all x0 -> x1, waiting for transfers between devices: none -> 116 us  [shards(): lax.all_to_all(jnp.stack([key_value_weight] * lax.axis_size('seq')), 'seq...]
    all_gather x1, waiting for transfers between devices: 147 us -> 245 us  [shards(): query_vectors = contract(lax.all_gather(w_query, 'seq', axis=0, tiled=True))]
    all_gather x1, waiting for transfers between devices: 44.6 us -> 0.02 us  [shards(): lax.all_gather(w_out, 'seq', axis=1, tiled=True)]
    all_to_all x0 -> x1, starting transfers between devices: none -> 19 us  [shards(): lax.all_to_all(jnp.stack([key_value_weight] * lax.axis_size('seq')), 'seq...]
    dot_general x0 -> x1, local copies, waits for them, and re-layouts: none -> 11.6 us  [contract(): return jnp.dot(normalized_input, piece, preferred_element_type=jnp.float32)]
    all_to_all x1, waiting for transfers between devices: 14.2 us -> 20.1 us  [shards(): lax.all_to_all(outgoing, 'seq', split_axis=0, concat_axis=0, tiled=True)]
  transfers between devices with their start and end apart: 8 -> 8, of which waited for: 8 -> 7; matrix products, arithmetic and copies ran while one was open for 9% -> 9% of each run, Pallas kernels for 0% -> 0%
where the time goes in v1:
time: 591 us; the launch traced here: 590 us
  waiting for transfers between devices  469 us (79%)
  local copies, waits for them, and re-layouts  37.9 us (6%)
  starting transfers between devices  36.9 us (6%)
  matrix products  22.5 us (4%)
  between operations  14.5 us (2%)
  other arithmetic  9.61 us (2%)
    all_gather x1, waiting for transfers between devices, shards(): query_vectors = contract(lax.all_gather(w_query, 'seq', axis=0, tiled=True))  245 us
    all_to_all x1, waiting for transfers between devices, shards(): lax.all_to_all(jnp.stack([key_value_weight] * lax.axis_size('seq')), 'seq...  116 us
    reduce_scatter x1, waiting for transfers between devices, shards(): lax.psum_scatter(partial_out.astype(jnp.bfloat16), 'tensor', scatter_dime...  30.4 us
    all_gather x1, waiting for transfers between devices, shards(): whole = lax.all_gather(hidden, 'tensor', axis=1, tiled=True)  27.8 us
    all_to_all x1, waiting for transfers between devices, shards(): lax.all_to_all(outgoing, 'seq', split_axis=0, concat_axis=0, tiled=True)  20.1 us
    all_to_all x1, starting transfers between devices, shards(): lax.all_to_all(jnp.stack([key_value_weight] * lax.axis_size('seq')), 'seq...  19 us
    all_to_all x1, waiting for transfers between devices, shards(): lax.all_to_all(out_block, 'seq', split_axis=0, concat_axis=0, tiled=True)  18.9 us
  transfers between devices with their start and end apart: 8, of which 7 were waited for; matrix products, arithmetic and copies ran while one was open for 9% of the time, Pallas kernels for 0%

profile of v1, /device:TPU:8, one launch (start us, length us, event | category | flops | bytes accessed | tf_op | source)
XLA Modules:
  0.0 590.4 jit_solution(9682956420404016576)
XLA Ops:
  7.2 5.2 stack.36
  12.4 19.0 %all-to-all-start.2 = ((bf16[64,64,1024]{2,1,0:T(8,128)(2,1)}), bf16[64,64,1024]{2,1,0:T(8,128)(2,1)}, u32[]{:S(2)}, u32[]{:S(2)}) async-start(bf16[64,64,1024]{2,1,0:T(8,128)(2,1)} %stack.36), calls=%async_computation.2 | async-start | bytes 16777216 | tf_op jit(solution)/shard_map/all_to_all | solution.py:84
  31.5 0.7 all-gather.4.cloned.1.call-update
  32.2 0.7 all-gather.6.cloned.1.call-update
  33.0 0.7 all-gather.8.cloned.1.call-update
  34.0 2.9 copy.123
  37.5 0.6 pad_clamp_fusion
  38.3 27.8 %all-gather.4.cloned.1.call-done = bf16[128,4096]{1,0:T(8,128)(2,1)} async-done(((bf16[128,512]{1,0:T(8,128)(2,1)}), bf16[128,4096]{1,0:T(8,128)(2,1)}) %all-gather.4.cloned.1.call-update) | async-done | bytes 1048592 | tf_op jit(solution)/shard_map/all_gather | solution.py:66
  66.2 1.5 fusion
  67.7 245.1 %all-gather.6.cloned.1.call-done = bf16[4096,512]{1,0:T(8,128)(2,1)} async-done(((bf16[64,512]{1,0:T(8,128)(2,1)}), bf16[4096,512]{1,0:T(8,128)(2,1)}) %all-gather.6.cloned.1.call-update) | async-done | bytes 4194320 | tf_op jit(solution)/shard_map/all_gather | solution.py:81
  312.8 4.3 fusion.18
  317.1 115.6 %all-to-all-done.2 = bf16[64,64,1024]{2,1,0:T(8,128)(2,1)} async-done(((bf16[64,64,1024]{2,1,0:T(8,128)(2,1)}), bf16[64,64,1024]{2,1,0:T(8,128)(2,1)}, u32[]{:S(2)}, u32[]{:S(2)}) %all-to-all-start.2) | async-done | bytes 8388640 | tf_op jit(solution)/shard_map/all_to_all | solution.py:84
  432.7 11.6 %copy.129 = bf16[1024,4096]{1,0:T(8,128)(2,1)} copy(bf16[1024,4096]{0,1:T(8,128)(2,1)} %bitcast.14) | data formatting | bytes 16777216 | tf_op jit(solution)/shard_map/dot_general | solution.py:79
  444.3 5.9 %fusion.11 = f32[128,4,2,128]{0,3,2,1:T(8,128)S(1)} fusion(bf16[4,2,128,4096]{3,2,1,0:T(8,128)(2,1)} %bitcast.157, bf16[128,4096]{1,0:T(8,128)(2,1)S(1)} %copy-done.6, f32[4096]{0:T(1024)S(1)} %convert_element_type.73, f32[128]{0:T(128)S(1)} %add_rsqrt_fusion), kind=kOutput, calls=%fused_computation.33 | convolution fusion | flops 1075838976 | bytes 9978368 | tf_op jit(solution)/shard_map/dot_general | solution.py:79
  450.5 1.2 gather_fusion
  451.8 0.9 broadcast_select_fusion
  452.6 5.7 all-to-all-start
  459.0 0.6 fusion.34
  460.3 0.6 fusion.33
  461.2 0.6 fusion.32
  461.8 0.8 convolution_bitcast_fusion
  462.5 20.1 %all-to-all-done = bf16[64,4,512]{2,1,0:T(4,128)(2,1)S(1)} async-done(((bf16[64,4,512]{2,1,0:T(4,128)(2,1)}), bf16[64,4,512]{2,1,0:T(4,128)(2,1)S(1)}, u32[]{:S(2)}, u32[]{:S(2)}) %all-to-all-start) | async-done | bytes 262176 | tf_op jit(solution)/shard_map/all_to_all | solution.py:122
  482.7 1.1 fusion.69
  484.8 0.6 copy-done.22
  485.9 0.8 add.239
  486.6 1.3 fusion.75
  487.9 1.0 copy-done
  490.3 1.4 add.237
  491.7 1.3 fusion.76
  492.9 1.0 copy-done.2
  494.8 0.6 add_convert_fusion.2
  495.4 1.4 add.235
  497.2 1.0 copy-done.4
  498.6 0.8 pad_maximum_fusion.1
  499.4 0.7 copy.125
  500.1 5.8 all-to-all-start.1
  505.9 1.1 fusion.6
  507.5 0.8 copy-done.3
  508.8 0.8 copy-done.5
  510.4 0.8 convert_element_type.83
  511.1 8.9 %all-to-all-done.1 = bf16[64,4,4]{1,2,0:T(4,128)(2,1)S(1)} async-done(((bf16[64,4,4]{1,2,0:T(4,128)(2,1)}), bf16[64,4,4]{1,2,0:T(4,128)(2,1)S(1)}, u32[]{:S(2)}, u32[]{:S(2)}) %all-to-all-start.1) | async-done | bytes 2080 | tf_op jit(solution)/shard_map/all_to_all | solution.py:139
  520.1 6.1 %all-to-all-start.3 = ((bf16[64,4,512]{2,1,0:T(4,128)(2,1)}), bf16[64,4,512]{2,1,0:T(4,128)(2,1)S(1)}, u32[]{:S(2)}, u32[]{:S(2)}) async-start(bf16[64,4,512]{2,1,0:T(4,128)(2,1)} %convert_element_type.83), calls=%async_computation.3 | async-start | bytes 524288 | tf_op jit(solution)/shard_map/all_to_all | solution.py:138
  527.1 0.8 gather_fusion.1
  528.0 18.9 %all-to-all-done.3 = bf16[64,4,512]{2,1,0:T(4,128)(2,1)S(1)} async-done(((bf16[64,4,512]{2,1,0:T(4,128)(2,1)}), bf16[64,4,512]{2,1,0:T(4,128)(2,1)S(1)}, u32[]{:S(2)}, u32[]{:S(2)}) %all-to-all-start.3) | async-done | bytes 262176 | tf_op jit(solution)/shard_map/all_to_all | solution.py:138
  547.0 0.9 gather_fusion.2
  548.1 4.6 convolution_convert_fusion
  552.8 0.7 copy.146
  553.5 30.4 %reduce-scatter.2.cloned.1.call-done = bf16[128,512]{1,0:T(8,128)(2,1)} async-done(((bf16[128,4096]{1,0:T(8,128)(2,1)}), bf16[128,512]{1,0:T(8,128)(2,1)}) %reduce-scatter.2.cloned.1.call-update) | async-done | bytes 131088 | tf_op jit(solution)/shard_map/reduce_scatter | solution.py:177
  (143 shorter events, 10.4 us)
Async XLA Ops:
  12.4 21.3 %copy-start.21 = (bf16[4096]{0:T(1024)(128)(2,1)S(1)}, bf16[4096]{0:T(1024)(128)(2,1)}, u32[]{:S(2)}) copy-start(bf16[4096]{0:T(1024)(128)(2,1)} %param.9) | copy-start | bytes 24580
  12.4 21.3 %copy-start.27 = (s32[1,64]{1,0:T(1,128)S(1)}, s32[1,64]{1,0:T(1,128)}, u32[]{:S(2)}) copy-start(s32[1,64]{1,0:T(1,128)} %param.15) | copy-start | bytes 772
  12.4 420.4 %all-to-all-start.2 = ((bf16[64,64,1024]{2,1,0:T(8,128)(2,1)}), bf16[64,64,1024]{2,1,0:T(8,128)(2,1)}, u32[]{:S(2)}, u32[]{:S(2)}) async-start(bf16[64,64,1024]{2,1,0:T(8,128)(2,1)} %stack.36), calls=%async_computation.2 | async-start | bytes 16777216 | tf_op jit(solution)/shard_map/all_to_all | solution.py:84
  31.4 34.8 %all-gather.4.cloned.1.call-start = ((), (), s32[]{:S(2)}) async-start(), calls=%async_computation.5 | async-start | bytes 1179648 | tf_op jit(solution)/shard_map/all_gather | solution.py:66
  32.2 280.7 %all-gather.6.cloned.1.call-start = ((), (), s32[]{:S(2)}) async-start(), calls=%async_computation.6 | async-start | bytes 4259840 | tf_op jit(solution)/shard_map/all_gather | solution.py:81
  32.9 515.2 %all-gather.8.cloned.1.call-start = ((), (), s32[]{:S(2)}) async-start(), calls=%async_computation.7 | async-start | bytes 4259840 | tf_op jit(solution)/shard_map/all_gather | solution.py:174
  34.0 2.9 copy-start.41
  432.7 11.6 %copy-start.6 = (bf16[128,4096]{1,0:T(8,128)(2,1)S(1)}, bf16[128,4096]{1,0:T(8,128)(2,1)}, u32[]{:S(2)}) copy-start(bf16[128,4096]{1,0:T(8,128)(2,1)} %all-gather.4.cloned.1.call-done) | copy-start | bytes 3145732
  452.6 30.0 %all-to-all-start = ((bf16[64,4,512]{2,1,0:T(4,128)(2,1)}), bf16[64,4,512]{2,1,0:T(4,128)(2,1)S(1)}, u32[]{:S(2)}, u32[]{:S(2)}) async-start(bf16[64,4,512]{2,1,0:T(4,128)(2,1)} %broadcast_select_fusion), calls=%async_computation | async-start | bytes 524288 | tf_op jit(solution)/shard_map/all_to_all | solution.py:122
  458.7 3.8 copy-start.28
  458.9 0.9 copy-start.30
  458.9 24.9 %copy-start.7 = (f32[128,128]{0,1:T(8,128)}, f32[128,128]{0,1:T(8,128)S(1)}, u32[]{:S(2)}) copy-start(f32[128,128]{0,1:T(8,128)S(1)} %get-tuple-element.24) | copy-start | bytes 196612
  459.0 3.5 copy-start.32
  459.8 24.0 %copy-start.9 = (f32[128,128]{0,1:T(8,128)}, f32[128,128]{0,1:T(8,128)S(1)}, u32[]{:S(2)}) copy-start(f32[128,128]{0,1:T(8,128)S(1)} %get-tuple-element.26) | copy-start | bytes 196612
  461.2 1.4 copy-start.11
  461.2 1.3 copy-start.38
  484.2 0.6 copy-start.14
  484.8 0.6 copy-start.22
  487.9 1.0 copy-start
  487.9 1.3 copy-start.15
  489.2 0.6 copy-start.23
  492.9 1.0 copy-start.2
  492.9 1.3 copy-start.17
  497.2 1.0 copy-start.4
  497.2 1.3 copy-start.19
  500.1 20.0 %all-to-all-start.1 = ((bf16[64,4,4]{1,2,0:T(4,128)(2,1)}), bf16[64,4,4]{1,2,0:T(4,128)(2,1)S(1)}, u32[]{:S(2)}, u32[]{:S(2)}) async-start(bf16[64,4,4]{1,2,0:T(4,128)(2,1)} %copy.125), calls=%async_computation.1 | async-start | bytes 131072 | tf_op jit(solution)/shard_map/all_to_all | solution.py:139
  505.9 1.2 copy-start.1
  505.9 1.2 copy-start.16
  505.9 1.2 copy-start.24
  507.1 1.2 copy-start.3
  507.1 1.2 copy-start.18
  507.1 1.2 copy-start.26
  508.4 1.2 copy-start.5
  508.4 1.2 copy-start.20
  510.0 16.3 %copy-start.8 = (f32[128,128]{0,1:T(8,128)S(1)}, f32[128,128]{0,1:T(8,128)}, u32[]{:S(2)}) copy-start(f32[128,128]{0,1:T(8,128)} %copy-done.7) | copy-start | bytes 196612
  510.0 16.3 %copy-start.31 = (f32[128]{0:T(128)S(1)}, f32[128]{0:T(128)}, u32[]{:S(2)}) copy-start(f32[128]{0:T(128)} %copy-done.30) | copy-start | bytes 1540
  510.0 16.3 %copy-start.36 = (f32[128]{0:T(128)S(1)}, f32[128]{0:T(128)}, u32[]{:S(2)}) copy-start(f32[128]{0:T(128)} %fusion.34) | copy-start | bytes 1540
  510.0 16.5 %copy-start.10 = (f32[128,128]{0,1:T(8,128)S(1)}, f32[128,128]{0,1:T(8,128)}, u32[]{:S(2)}) copy-start(f32[128,128]{0,1:T(8,128)} %copy-done.9) | copy-start | bytes 196612
  510.0 16.5 %copy-start.35 = (f32[128]{0:T(128)S(1)}, f32[128]{0:T(128)}, u32[]{:S(2)}) copy-start(f32[128]{0:T(128)} %copy-done.34) | copy-start | bytes 1540
  510.0 16.5 %copy-start.37 = (f32[128]{0:T(128)S(1)}, f32[128]{0:T(128)}, u32[]{:S(2)}) copy-start(f32[128]{0:T(128)} %fusion.33) | copy-start | bytes 1540
  510.0 16.6 %copy-start.12 = (f32[128,128]{0,1:T(8,128)S(1)}, f32[128,128]{0,1:T(8,128)}, u32[]{:S(2)}) copy-start(f32[128,128]{0,1:T(8,128)} %copy-done.11) | copy-start | bytes 196612
  510.0 16.6 %copy-start.39 = (f32[128]{0:T(128)S(1)}, f32[128]{0:T(128)}, u32[]{:S(2)}) copy-start(f32[128]{0:T(128)} %copy-done.38) | copy-start | bytes 1540
  510.1 16.6 %copy-start.40 = (f32[128]{0:T(128)S(1)}, f32[128]{0:T(128)}, u32[]{:S(2)}) copy-start(f32[128]{0:T(128)} %fusion.32) | copy-start | bytes 1540
  510.1 16.7 %copy-start.29 = (f32[128]{0:T(128)S(1)}, f32[128]{0:T(128)}, u32[]{:S(2)}) copy-start(f32[128]{0:T(128)} %copy-done.28) | copy-start | bytes 1540
  510.1 16.7 %copy-start.33 = (f32[128]{0:T(128)S(1)}, f32[128]{0:T(128)}, u32[]{:S(2)}) copy-start(f32[128]{0:T(128)} %copy-done.32) | copy-start | bytes 1540
  510.1 37.8 %copy-start.13 = (f32[128,1,128]{0,2,1:T(8,128)S(1)}, f32[128,1,128]{0,2,1:T(8,128)}, u32[]{:S(2)}) copy-start(f32[128,1,128]{0,2,1:T(8,128)} %convolution_bitcast_fusion) | copy-start | bytes 196612
  520.1 26.8 %all-to-all-start.3 = ((bf16[64,4,512]{2,1,0:T(4,128)(2,1)}), bf16[64,4,512]{2,1,0:T(4,128)(2,1)S(1)}, u32[]{:S(2)}, u32[]{:S(2)}) async-start(bf16[64,4,512]{2,1,0:T(4,128)(2,1)} %convert_element_type.83), calls=%async_computation.3 | async-start | bytes 524288 | tf_op jit(solution)/shard_map/all_to_all | solution.py:138
  526.2 57.6 %reduce-scatter.2.cloned.1.call-start = ((), (), s32[]{:S(2)}) async-start(), calls=%async_computation.8 | async-start | bytes 1179648 | tf_op jit(solution)/shard_map/reduce_scatter | solution.py:177
  (2 other events, 1.0 us)
Sparse Core Ops, SparseCore 0:
  34.4 31.7 all-gather.3
  69.1 243.6 all-gather.5
  315.8 188.8 all-gather.7
  552.9 30.9 reduce-scatter.1
